TPU v7x, 256 devices: a whole 4x4x8 slice. The times are simulated.
256 devices in a mesh: space: 32 (over z, x), mode: 8 (over y, core).
Axes of the slice: x: 4, y: 4, z: 8, core: 2. Of those that a mesh axis runs over, the one named last changes fastest.
Arguments:
- vectors: float32 [55296, 256], P('space', 'mode'), may hold values from -6 to 6
- force_blocks: float32 [288, 27, 192, 192], P('space', None, 'mode'), as said below
- inverse_blocks: float32 [288, 192, 192], P('space'), as said below
- neighbours: int32 [288, 27], P('space'), may hold values from 0 to 287, as said below
Outputs:
- w_block: float32 [55296, 256], P('space', 'mode')
- hw_block: float32 [55296, 256], P('space', 'mode')
- gram_a: float32 [512, 2, 256], P(None, None, 'mode')
- gram_b: float32 [512, 2, 256], P(None, None, 'mode')
Inputs may be any that keep to these rules, and one draw needn't show every extreme that they name: `neighbours`: block rows are atom cells on a periodic grid of 32 layers of 3 x 3 cells; the rows of layer z are z * 9 to z * 9 + 8 in some order. Entry k = 9 (dz + 1) + 3 (dy + 1) + (dx + 1) of row i is the block row of the cell at offset (dz, dy, dx) from row i's cell, so entry 13 is i itself. H is symmetric: force_blocks[neighbours[i, k], 26 - k] is the transpose of force_blocks[i, k]. `inverse_blocks`: every block is symmetric.
All inputs are finite; a program needn't handle non-finite values.
Results may differ from a plain program's by a relative error of at most 0.00013.
Values sent between devices are 32-bit elements; how exact they have to be, the bound alone decides.
No kernel may reach another device: no remote copies, remote signals or barrier semaphores. Data moves between devices by JAX's collectives and lax.ppermute only.
A program may use at most 128 MiB of HBM per device.

v0:
```python
import jax
import jax.numpy as jnp
from jax import lax
from jax.sharding import PartitionSpec as P

CELLS = 9
HIGHEST = lax.Precision.HIGHEST


def space_sum(value):
    count = lax.axis_size("space")
    step = 1
    while step < count:
        pairs = [(i, i ^ step) for i in range(count)]
        value = value + lax.ppermute(value, "space", pairs)
        step *= 2
    return value


def halo(block, width):
    count = lax.axis_size("space")
    forward = [(i, (i + 1) % count) for i in range(count)]
    backward = [((i + 1) % count, i) for i in range(count)]
    low = lax.ppermute(block[block.shape[0] - width :], "space", forward)
    high = lax.ppermute(block[:width], "space", backward)
    return (low, high)


def dense_rows(force_blocks, local_ids, ext_blocks):
    block_rows, neigh = local_ids.shape
    columns = jnp.arange(ext_blocks, dtype=jnp.int32)
    onehot = local_ids[:, :, None] == columns[None, None, :]
    offsets = jnp.arange(neigh, dtype=jnp.int32)
    which = jnp.sum(jnp.where(onehot, offsets[None, :, None], 0), axis=1)
    valid = jnp.any(onehot, axis=1)
    flat = (jnp.arange(block_rows, dtype=jnp.int32)[:, None] * neigh + which).reshape(-1)
    rows, cols = (force_blocks.shape[2], force_blocks.shape[3])
    table = force_blocks.reshape(block_rows * neigh, rows * cols)
    picked = jnp.take(table, flat, axis=0).reshape(block_rows, ext_blocks, rows, cols)
    return jnp.where(valid[:, :, None, None], picked, 0.0)


def apply_dense(dense, low, own, high):
    width = low.shape[0]
    own_count = own.shape[0]
    parts = (
        (dense[:, width : width + own_count], own),
        (dense[:, :width], low),
        (dense[:, width + own_count :], high),
    )
    total = None
    for coeffs, field in parts:
        product = jnp.einsum(
            "ijrc,jcm->irm", coeffs, field, precision=HIGHEST, preferred_element_type=jnp.float32
        )
        total = product if total is None else total + product
    regrouped = lax.all_to_all(total, "mode", split_axis=2, concat_axis=1, tiled=True)
    return regrouped.reshape(-1, regrouped.shape[2])


def local(vectors, force_blocks, inverse_blocks, neighbours):
    row_count, col_count = vectors.shape
    block_size = inverse_blocks.shape[1]
    block_rows = row_count // block_size
    slab_count = lax.axis_size("space")
    total_rows = row_count * slab_count
    own_layers = block_rows // CELLS
    layer_total = own_layers * slab_count
    slab_index = lax.axis_index("space")
    mode_index = lax.axis_index("mode")
    layer_of = neighbours // CELLS
    relative = (layer_of - slab_index * own_layers + 1) % layer_total
    local_ids = relative * CELLS + neighbours % CELLS
    ext_blocks = block_rows + 2 * CELLS
    dense = dense_rows(force_blocks, local_ids, ext_blocks)
    stacked_x = vectors.reshape(block_rows, block_size, col_count)
    full_x = lax.all_gather(stacked_x, "mode", axis=2, tiled=True)
    low_x, high_x = halo(full_x, CELLS)
    image_x = apply_dense(dense, low_x, full_x, high_x)
    mode_count = full_x.shape[2]
    flat_x = full_x.reshape(row_count, mode_count)
    rayleigh = (
        space_sum(
            jnp.einsum(
                "ra,rj->aj", flat_x, image_x, precision=HIGHEST, preferred_element_type=jnp.float32
            )
        )
        / total_rows
    )
    residual = image_x - jnp.dot(
        flat_x, rayleigh, precision=HIGHEST, preferred_element_type=jnp.float32
    )
    search_raw = jnp.einsum(
        "brc,bcm->brm",
        inverse_blocks,
        residual.reshape(block_rows, block_size, col_count),
        precision=HIGHEST,
        preferred_element_type=jnp.float32,
    )
    full_s = lax.all_gather(search_raw, "mode", axis=2, tiled=True)
    low_s, high_s = halo(full_s, CELLS)
    image_s = apply_dense(dense, low_s, full_s, high_s)
    flat_s = full_s.reshape(row_count, mode_count)
    own_s = search_raw.reshape(row_count, col_count)
    squares = jnp.sum(flat_s * flat_s, axis=0)
    basis = jnp.concatenate([flat_x, flat_s], axis=1)
    columns = jnp.stack([vectors, own_s, image_x, image_s], axis=1)
    gram_part = jnp.einsum(
        "ra,rgj->agj", basis, columns, precision=HIGHEST, preferred_element_type=jnp.float32
    )
    packed = jnp.concatenate([gram_part.reshape(-1), squares])
    summed = space_sum(packed)
    gram_sum = summed[: gram_part.size].reshape(gram_part.shape)
    scales_all = lax.rsqrt(summed[gram_part.size :] / total_rows + 1e-06)
    scales_own = lax.dynamic_slice_in_dim(scales_all, mode_index * col_count, col_count)
    w_block = own_s * scales_own
    hw_block = image_s * scales_own
    row_scale = jnp.concatenate([jnp.ones((mode_count,), jnp.float32), scales_all])
    ones_own = jnp.ones((col_count,), jnp.float32)
    col_scale = jnp.stack([ones_own, scales_own, ones_own, scales_own])
    gram = gram_sum * row_scale[:, None, None] * col_scale[None] / total_rows
    gram_b = gram[:, 0:2]
    gram_a = gram[:, 2:4]
    return (w_block, hw_block, gram_a, gram_b)


def solution(mesh):
    in_specs = (
        P("space", "mode"),
        P("space", None, "mode", None),
        P("space", None, None),
        P("space", None),
    )
    out_specs = (
        P("space", "mode"),
        P("space", "mode"),
        P(None, None, "mode"),
        P(None, None, "mode"),
    )
    return jax.shard_map(local, mesh=mesh, in_specs=in_specs, out_specs=out_specs, check_vma=False)
```

profile of v0, /device:TPU:2, one launch (start us, length us, event | category | flops | bytes accessed | tf_op | source)
XLA Modules:
  0.0 340.8 jit_solution(18224668722310381705)
XLA Ops:
  9.4 31.6 %all-gather.3.cloned.1.call-done = f32[9,192,256]{1,2,0:T(8,128)} async-done(((f32[9,192,32]{1,2,0:T(8,128)}), f32[9,192,256]{1,2,0:T(8,128)}) %all-gather.3.cloned.1.call-update) | async-done | bytes 1769488 | tf_op jit(solution)/shard_map/all_gather | solution.py:77
  46.7 6.7 %reshape.102 = f32[243,4608]{1,0:T(8,128)} reshape(f32[9,27,24,192]{3,2,1,0:T(8,128)} %param.5) | data formatting | bytes 8957952 | tf_op jit(solution)/shard_map/reshape | solution.py:38
  53.5 8.4 %gather_fusion = f32[243,4608]{1,0:T(8,128)} fusion(f32[243,4608]{1,0:T(8,128)} %reshape.102, s32[1024]{0:T(1024)S(1)} %pad_clamp_fusion), kind=kCustom, calls=%fused_computation | custom fusion | bytes 8958924 | tf_op jit(solution)/shard_map/jit(_take)/gather | solution.py:39
  61.9 6.9 %gather.7 = f32[9,27,24,192]{3,2,1,0:T(8,128)} reshape(f32[243,4608]{1,0:T(8,128)} %gather_fusion) | data formatting | bytes 8957952 | tf_op jit(solution)/shard_map/jit(_take)/gather | solution.py:39
  68.9 4.6 %fusion.19 = f32[9,24,256]{2,1,0:T(8,128)S(1)} fusion(f32[9,192,256]{1,2,0:T(8,128)} %all-gather.3.cloned.1.call-done, f32[9,27,24,192]{3,2,1,0:T(8,128)} %gather.7, pred[9,27]{1,0:T(8,128)(4,1)S(1)} %get-tuple-element.16, pred[9,27]{1,0:T(8,128)(4,1)S(1)} %fusion.47), kind=kOutput, calls=%fused_computation.25 | convolution fusion | flops 1148857344 | bytes 6470118 | tf_op jit(solution)/shard_map/ijrc,jcm->irm/dot_general | solution.py:53
  73.5 10.4 %collective-permute-done = f32[9,192,256]{2,1,0:T(8,128)} collective-permute-done((f32[9,192,256]{2,1,0:T(8,128)S(1)}, f32[9,192,256]{2,1,0:T(8,128)}, u32[]{:S(2)}, u32[]{:S(2)}) %collective-permute-start) | collective-permute-done | bytes 1769504 | tf_op jit(solution)/shard_map/ppermute | solution.py:24
  87.4 4.2 %fusion.34 = f32[9,24,256]{2,1,0:T(8,128)} fusion(f32[9,24,256]{2,1,0:T(8,128)S(1)} %fusion.37, f32[9,192,256]{2,1,0:T(8,128)} %collective-permute-done.1, f32[9,27,24,192]{3,2,1,0:T(8,128)S(1)} %copy-done.1, pred[9,27]{1,0:T(8,128)(4,1)S(1)} %get-tuple-element.16, pred[9,27]{1,0:T(8,128)(4,1)S(1)} %fusion.47), kind=kOutput, calls=%fused_computation.30 | convolution fusion | flops 1148912640 | bytes 6691302 | tf_op jit(solution)/shard_map/ijrc,jcm->irm/dot_general | solution.py:53
  98.1 11.1 %all_to_all.30 = f32[8,1,6912]{2,1,0:T(1,128)} all-to-all(f32[8,1,6912]{2,1,0:T(1,128)} %reshape.133), channel_id=1, replica_groups=mesh['space'=32,'mode'=8] {'mode'}, dimensions={0} | all-to-all | bytes 442368 | tf_op jit(solution)/shard_map/all_to_all | solution.py:57
  122.8 4.3 %collective-permute-start.2 = (f32[256,32]{0,1:T(8,128)S(1)}, f32[256,32]{0,1:T(8,128)S(1)}, u32[]{:S(2)}, u32[]{:S(2)}) collective-permute-start(f32[256,32]{0,1:T(8,128)S(1)} %convolution_bitcast_fusion.3), channel_id=1, source_target_pairs={{0,8},{8,0},{16,24},{24,16},{32,40},{40,32},{48,56},{56,48},{64,72... | collective-permute-start | bytes 98312 | tf_op jit(solution)/shard_map/ppermute | solution.py:15
  129.1 5.4 %collective-permute-done.3 = f32[256,32]{0,1:T(8,128)S(1)} collective-permute-done((f32[256,32]{0,1:T(8,128)S(1)}, f32[256,32]{0,1:T(8,128)S(1)}, u32[]{:S(2)}, u32[]{:S(2)}) %collective-permute-start.3) | collective-permute-done | bytes 32800 | tf_op jit(solution)/shard_map/ppermute | solution.py:15
  143.4 5.4 %collective-permute-start.6 = (f32[256,32]{0,1:T(8,128)S(1)}, f32[256,32]{0,1:T(8,128)S(1)}, u32[]{:S(2)}, u32[]{:S(2)}) collective-permute-start(f32[256,32]{0,1:T(8,128)S(1)} %add.131), channel_id=1, source_target_pairs={{0,128},{8,136},{16,144},{24,152},{32,160},{40,168},{48,176},{56,1... | collective-permute-start | bytes 98312 | tf_op jit(solution)/shard_map/ppermute | solution.py:15
  157.1 26.9 %all-gather.5.cloned.1.call-done = f32[9,192,256]{1,2,0:T(8,128)} async-done(((f32[9,192,32]{1,2,0:T(8,128)}), f32[9,192,256]{1,2,0:T(8,128)}) %all-gather.5.cloned.1.call-update) | async-done | bytes 1769488 | tf_op jit(solution)/shard_map/all_gather | solution.py:100
  193.2 4.6 %fusion.16 = f32[9,24,256]{2,1,0:T(8,128)S(1)} fusion(f32[9,192,256]{1,2,0:T(8,128)} %all-gather.5.cloned.1.call-done, f32[9,27,24,192]{3,2,1,0:T(8,128)} %gather.7, pred[9,27]{1,0:T(8,128)(4,1)S(1)} %get-tuple-element.16, pred[9,27]{1,0:T(8,128)(4,1)S(1)} %fusion.47), kind=kOutput, calls=%fused_computation.24 | convolution fusion | flops 1148857344 | bytes 6470118 | tf_op jit(solution)/shard_map/ijrc,jcm->irm/dot_general | solution.py:53
  197.9 30.2 %collective-permute-done.7 = f32[9,192,256]{2,1,0:T(8,128)} collective-permute-done((f32[9,192,256]{2,1,0:T(8,128)}, f32[9,192,256]{2,1,0:T(8,128)}, u32[]{:S(2)}, u32[]{:S(2)}) %collective-permute-start.7) | collective-permute-done | bytes 1769504 | tf_op jit(solution)/shard_map/ppermute | solution.py:24
  232.1 4.1 %fusion.40 = f32[9,24,256]{2,1,0:T(8,128)} fusion(f32[9,24,256]{2,1,0:T(8,128)S(1)} %fusion.43, f32[9,192,256]{2,1,0:T(8,128)} %collective-permute-done.8, f32[9,27,24,192]{3,2,1,0:T(8,128)S(1)} %bitcast.126, pred[9,27]{1,0:T(8,128)(4,1)S(1)} %get-tuple-element.16, pred[9,27]{1,0:T(8,128)(4,1)S(1)} %fusion.47), kind=kOutput, calls=%fused_computation.32 | convolution fusion | flops 1148912640 | bytes 6691302 | tf_op jit(solution)/shard_map/ijrc,jcm->irm/dot_general | solution.py:53
  248.5 5.1 %all-to-all-done.1 = f32[8,1,6912]{2,1,0:T(1,128)S(1)} async-done(((f32[8,1,6912]{2,1,0:T(1,128)}), f32[8,1,6912]{2,1,0:T(1,128)S(1)}, u32[]{:S(2)}, u32[]{:S(2)}) %all-to-all-start.1) | async-done | bytes 221216 | tf_op jit(solution)/shard_map/all_to_all | solution.py:57
  263.7 7.3 %convolution_bitcast_fusion = f32[65536]{0:T(1024)S(1)} fusion(f32[1728,128]{0,1:T(8,128)S(1)} %bitcast.139, f32[1728,256]{1,0:T(8,128)} %bitcast.138, f32[1728,256]{1,0:T(8,128)S(1)} %bitcast.129), kind=kOutput, calls=%fused_computation.1 | convolution fusion | flops 1359839232 | bytes 4685824
  271.1 4.3 %collective-permute-start.9 = (f32[65792]{0:T(1024)S(1)}, f32[65792]{0:T(1024)S(1)}, u32[]{:S(2)}, u32[]{:S(2)}) collective-permute-start(f32[65792]{0:T(1024)S(1)} %pad_maximum_fusion.1), channel_id=1, source_target_pairs={{0,8},{8,0},{16,24},{24,16},{32,40},{40,32},{48,56},{56,48},{64,72... | collective-permute-start | bytes 789512 | tf_op jit(solution)/shard_map/ppermute | solution.py:15
  275.5 6.1 %collective-permute-done.9 = f32[65792]{0:T(1024)S(1)} collective-permute-done((f32[65792]{0:T(1024)S(1)}, f32[65792]{0:T(1024)S(1)}, u32[]{:S(2)}, u32[]{:S(2)}) %collective-permute-start.9) | collective-permute-done | bytes 263200 | tf_op jit(solution)/shard_map/ppermute | solution.py:15
  281.7 8.7 %collective-permute-done.10 = f32[65792]{0:T(1024)S(1)} collective-permute-done((f32[65792]{0:T(1024)S(1)}, f32[65792]{0:T(1024)S(1)}, u32[]{:S(2)}, u32[]{:S(2)}) %collective-permute-start.10) | collective-permute-done | bytes 263200 | tf_op jit(solution)/shard_map/ppermute | solution.py:15
  290.6 6.4 %collective-permute-done.11 = f32[65792]{0:T(1024)S(1)} collective-permute-done((f32[65792]{0:T(1024)S(1)}, f32[65792]{0:T(1024)S(1)}, u32[]{:S(2)}, u32[]{:S(2)}) %collective-permute-start.11) | collective-permute-done | bytes 263200 | tf_op jit(solution)/shard_map/ppermute | solution.py:15
  298.1 10.9 %collective-permute-done.12 = f32[65792]{0:T(1024)S(1)} collective-permute-done((f32[65792]{0:T(1024)S(1)}, f32[65792]{0:T(1024)S(1)}, u32[]{:S(2)}, u32[]{:S(2)}) %collective-permute-start.12) | collective-permute-done | bytes 263200 | tf_op jit(solution)/shard_map/ppermute | solution.py:15
  309.7 5.6 %collective-permute-start.13 = (f32[65792]{0:T(1024)}, f32[65792]{0:T(1024)}, u32[]{:S(2)}, u32[]{:S(2)}) collective-permute-start(f32[65792]{0:T(1024)} %add.138), channel_id=1, source_target_pairs={{0,128},{8,136},{16,144},{24,152},{32,160},{40,168},{48,176},{56,1... | collective-permute-start | bytes 789512 | tf_op jit(solution)/shard_map/ppermute | solution.py:15
  316.5 10.9 %collective-permute-done.13 = f32[65792]{0:T(1024)} collective-permute-done((f32[65792]{0:T(1024)}, f32[65792]{0:T(1024)}, u32[]{:S(2)}, u32[]{:S(2)}) %collective-permute-start.13) | collective-permute-done | bytes 263200 | tf_op jit(solution)/shard_map/ppermute | solution.py:15
  (109 shorter events, 95.8 us)
Async XLA Ops:
  7.2 147.5 %copy-start = (f32[9,192,192]{2,1,0:T(8,128)S(1)}, f32[9,192,192]{2,1,0:T(8,128)}, u32[]{:S(2)}) copy-start(f32[9,192,192]{2,1,0:T(8,128)} %param.6) | copy-start | bytes 3981316
  7.2 33.8 %all-gather.3.cloned.1.call-start = ((), (), s32[]{:S(2)}) async-start(), calls=%async_computation.2 | async-start | bytes 2654208 | tf_op jit(solution)/shard_map/all_gather | solution.py:77
  9.3 35.8 %copy-start.10 = (s32[9,27]{1,0:T(8,128)S(1)}, s32[9,27]{1,0:T(8,128)}, u32[]{:S(2)}) copy-start(s32[9,27]{1,0:T(8,128)} %param.7) | copy-start | bytes 2920
  9.3 174.6 %all-gather.5.cloned.1.call-start = ((), (), s32[]{:S(2)}) async-start(), calls=%async_computation.3 | async-start | bytes 2654208 | tf_op jit(solution)/shard_map/all_gather | solution.py:100
  43.0 108.2 %copy-start.2 = (f32[9,192,256]{2,1,0:T(8,128)}, f32[9,192,256]{2,1,0:T(8,128)S(1)}, u32[]{:S(2)}) copy-start(f32[9,192,256]{2,1,0:T(8,128)S(1)} %copy.50) | copy-start | bytes 5308420
  43.0 40.9 %collective-permute-start = (f32[9,192,256]{2,1,0:T(8,128)S(1)}, f32[9,192,256]{2,1,0:T(8,128)}, u32[]{:S(2)}, u32[]{:S(2)}) collective-permute-start(f32[9,192,256]{2,1,0:T(8,128)S(1)} %copy.50), channel_id=1, source_target_pairs={{0,8},{8,16},{16,24},{24,32},{32,40},{40,48},{48,56},{56,64},{64,7... | collective-permute-start | bytes 5308424 | tf_op jit(solution)/shard_map/ppermute | solution.py:24
  44.6 42.8 %collective-permute-start.1 = (f32[9,192,256]{2,1,0:T(8,128)S(1)}, f32[9,192,256]{2,1,0:T(8,128)}, u32[]{:S(2)}, u32[]{:S(2)}) collective-permute-start(f32[9,192,256]{2,1,0:T(8,128)S(1)} %copy.50), channel_id=1, source_target_pairs={{8,0},{16,8},{24,16},{32,24},{40,32},{48,40},{56,48},{64,56},{72,6... | collective-permute-start | bytes 5308424 | tf_op jit(solution)/shard_map/ppermute | solution.py:25
  122.8 6.2 %collective-permute-start.2 = (f32[256,32]{0,1:T(8,128)S(1)}, f32[256,32]{0,1:T(8,128)S(1)}, u32[]{:S(2)}, u32[]{:S(2)}) collective-permute-start(f32[256,32]{0,1:T(8,128)S(1)} %convolution_bitcast_fusion.3), channel_id=1, source_target_pairs={{0,8},{8,0},{16,24},{24,16},{32,40},{40,32},{48,56},{56,48},{64,72... | collective-permute-start | bytes 98312 | tf_op jit(solution)/shard_map/ppermute | solution.py:15
  129.1 5.4 %collective-permute-start.3 = (f32[256,32]{0,1:T(8,128)S(1)}, f32[256,32]{0,1:T(8,128)S(1)}, u32[]{:S(2)}, u32[]{:S(2)}) collective-permute-start(f32[256,32]{0,1:T(8,128)S(1)} %add.128), channel_id=1, source_target_pairs={{0,16},{8,24},{16,0},{24,8},{32,48},{40,56},{48,32},{56,40},{64,80... | collective-permute-start | bytes 98312 | tf_op jit(solution)/shard_map/ppermute | solution.py:15
  134.5 4.1 %collective-permute-start.4 = (f32[256,32]{0,1:T(8,128)S(1)}, f32[256,32]{0,1:T(8,128)S(1)}, u32[]{:S(2)}, u32[]{:S(2)}) collective-permute-start(f32[256,32]{0,1:T(8,128)S(1)} %add.129), channel_id=1, source_target_pairs={{0,32},{8,40},{16,48},{24,56},{32,0},{40,8},{48,16},{56,24},{64,96... | collective-permute-start | bytes 98312 | tf_op jit(solution)/shard_map/ppermute | solution.py:15
  138.6 4.8 %collective-permute-start.5 = (f32[256,32]{0,1:T(8,128)S(1)}, f32[256,32]{0,1:T(8,128)S(1)}, u32[]{:S(2)}, u32[]{:S(2)}) collective-permute-start(f32[256,32]{0,1:T(8,128)S(1)} %add.130), channel_id=1, source_target_pairs={{0,64},{8,72},{16,80},{24,88},{32,96},{40,104},{48,112},{56,120},{... | collective-permute-start | bytes 98312 | tf_op jit(solution)/shard_map/ppermute | solution.py:15
  143.4 7.8 %collective-permute-start.6 = (f32[256,32]{0,1:T(8,128)S(1)}, f32[256,32]{0,1:T(8,128)S(1)}, u32[]{:S(2)}, u32[]{:S(2)}) collective-permute-start(f32[256,32]{0,1:T(8,128)S(1)} %add.131), channel_id=1, source_target_pairs={{0,128},{8,136},{16,144},{24,152},{32,160},{40,168},{48,176},{56,1... | collective-permute-start | bytes 98312 | tf_op jit(solution)/shard_map/ppermute | solution.py:15
  187.0 41.1 %collective-permute-start.7 = (f32[9,192,256]{2,1,0:T(8,128)}, f32[9,192,256]{2,1,0:T(8,128)}, u32[]{:S(2)}, u32[]{:S(2)}) collective-permute-start(f32[9,192,256]{2,1,0:T(8,128)} %copy.57), channel_id=1, source_target_pairs={{0,8},{8,16},{16,24},{24,32},{32,40},{40,48},{48,56},{56,64},{64,7... | collective-permute-start | bytes 5308424 | tf_op jit(solution)/shard_map/ppermute | solution.py:24
  188.4 43.6 %collective-permute-start.8 = (f32[9,192,256]{2,1,0:T(8,128)}, f32[9,192,256]{2,1,0:T(8,128)}, u32[]{:S(2)}, u32[]{:S(2)}) collective-permute-start(f32[9,192,256]{2,1,0:T(8,128)} %copy.57), channel_id=1, source_target_pairs={{8,0},{16,8},{24,16},{32,24},{40,32},{48,40},{56,48},{64,56},{72,6... | collective-permute-start | bytes 5308424 | tf_op jit(solution)/shard_map/ppermute | solution.py:25
  191.2 40.9 %slice-start = ((s8[5971968]{0:T(1024)(128)(4,1)}), s8[1777664]{0:T(1024)(128)(4,1)S(1)}, s32[]{:S(2)}) async-start(s8[5971968]{0:T(1024)(128)(4,1)} %bitcast.125), calls=%async_computation.4 | async-start | bytes 3555328
  193.2 38.9 %slice-start.1 = ((s8[5971968]{0:T(1024)(128)(4,1)}), s8[4194304]{0:T(1024)(128)(4,1)S(1)}, s32[]{:S(2)}) async-start(s8[5971968]{0:T(1024)(128)(4,1)} %bitcast.125), calls=%async_computation.5 | async-start | bytes 8388608
  242.7 10.9 %all-to-all-start.1 = ((f32[8,1,6912]{2,1,0:T(1,128)}), f32[8,1,6912]{2,1,0:T(1,128)S(1)}, u32[]{:S(2)}, u32[]{:S(2)}) async-start(f32[8,1,6912]{2,1,0:T(1,128)} %reshape.135), calls=%async_computation.1 | async-start | bytes 442368 | tf_op jit(solution)/shard_map/all_to_all | solution.py:57
  271.1 44.2 %copy-start.6 = (f32[9,192,32]{1,0,2:T(8,128)S(1)}, f32[9,192,32]{1,0,2:T(8,128)}, u32[]{:S(2)}) copy-start(f32[9,192,32]{1,0,2:T(8,128)} %copy.56) | copy-start | bytes 663556
  271.1 45.1 %copy-start.5 = (f32[9,24,8,32]{1,2,0,3:T(8,128)S(1)}, f32[9,24,8,32]{1,2,0,3:T(8,128)}, u32[]{:S(2)}) copy-start(f32[9,24,8,32]{1,2,0,3:T(8,128)} %copy.76) | copy-start | bytes 663556
  271.1 10.4 %collective-permute-start.9 = (f32[65792]{0:T(1024)S(1)}, f32[65792]{0:T(1024)S(1)}, u32[]{:S(2)}, u32[]{:S(2)}) collective-permute-start(f32[65792]{0:T(1024)S(1)} %pad_maximum_fusion.1), channel_id=1, source_target_pairs={{0,8},{8,0},{16,24},{24,16},{32,40},{40,32},{48,56},{56,48},{64,72... | collective-permute-start | bytes 789512 | tf_op jit(solution)/shard_map/ppermute | solution.py:15
  281.6 8.8 %collective-permute-start.10 = (f32[65792]{0:T(1024)S(1)}, f32[65792]{0:T(1024)S(1)}, u32[]{:S(2)}, u32[]{:S(2)}) collective-permute-start(f32[65792]{0:T(1024)S(1)} %fusion.73), channel_id=1, source_target_pairs={{0,16},{8,24},{16,0},{24,8},{32,48},{40,56},{48,32},{56,40},{64,80... | collective-permute-start | bytes 789512 | tf_op jit(solution)/shard_map/ppermute | solution.py:15
  290.5 6.5 %collective-permute-start.11 = (f32[65792]{0:T(1024)S(1)}, f32[65792]{0:T(1024)S(1)}, u32[]{:S(2)}, u32[]{:S(2)}) collective-permute-start(f32[65792]{0:T(1024)S(1)} %add.136), channel_id=1, source_target_pairs={{0,32},{8,40},{16,48},{24,56},{32,0},{40,8},{48,16},{56,24},{64,96... | collective-permute-start | bytes 789512 | tf_op jit(solution)/shard_map/ppermute | solution.py:15
  297.0 11.9 %collective-permute-start.12 = (f32[65792]{0:T(1024)S(1)}, f32[65792]{0:T(1024)S(1)}, u32[]{:S(2)}, u32[]{:S(2)}) collective-permute-start(f32[65792]{0:T(1024)S(1)} %add.137), channel_id=1, source_target_pairs={{0,64},{8,72},{16,80},{24,88},{32,96},{40,104},{48,112},{56,120},{... | collective-permute-start | bytes 789512 | tf_op jit(solution)/shard_map/ppermute | solution.py:15
  309.7 17.7 %collective-permute-start.13 = (f32[65792]{0:T(1024)}, f32[65792]{0:T(1024)}, u32[]{:S(2)}, u32[]{:S(2)}) collective-permute-start(f32[65792]{0:T(1024)} %add.138), channel_id=1, source_target_pairs={{0,128},{8,136},{16,144},{24,152},{32,160},{40,168},{48,176},{56,1... | collective-permute-start | bytes 789512 | tf_op jit(solution)/shard_map/ppermute | solution.py:15
  (6 other events, 118.1 us)
Sparse Core Ops, SparseCore 0:
  9.8 31.0 all-gather.2
  157.2 26.6 all-gather.4
where the time goes:
time: 348 us; the launch traced here: 341 us
  waiting for transfers between devices  165 us (47%)
  local copies, waits for them, and re-layouts  68.5 us (20%)
  matrix products  39.1 us (11%)
  starting transfers between devices  30.3 us (9%)
  between operations  14.7 us (4%)
  other arithmetic  12.6 us (4%)
  blocking collectives  11.1 us (3%)
    ppermute x10, waiting for transfers between devices, space_sum(): value = value + lax.ppermute(value, 'space', pairs)  60.5 us
    ppermute x2, waiting for transfers between devices, halo(): low = lax.ppermute(block[block.shape[0] - width:], 'space', forward)  40.6 us
    all_gather x1, waiting for transfers between devices, local(): full_x = lax.all_gather(stacked_x, 'mode', axis=2, tiled=True)  31.6 us
    all_gather x1, waiting for transfers between devices, local(): full_s = lax.all_gather(search_raw, 'mode', axis=2, tiled=True)  26.9 us
    dot_general x6, matrix products, apply_dense(): jnp.einsum('ijrc,jcm->irm', coeffs, field, precision=HIGHEST, preferred_e...  25 us
    ppermute x10, starting transfers between devices, space_sum(): value = value + lax.ppermute(value, 'space', pairs)  22.1 us
    gather x2, local copies, waits for them, and re-layouts, dense_rows(): jnp.take(table, flat, axis=0).reshape(block_rows, ext_blocks, rows, cols)  15.3 us
    unnamed x32, local copies, waits for them, and re-layouts  12.6 us
  transfers between devices with their start and end apart: 17, of which 15 were waited for; matrix products, arithmetic and copies ran while one was open for 14% of the time, Pallas kernels for 0%

commit v1 on v0

--- a/solution.py
+++ b/solution.py
@@ -97,7 +97,9 @@
         precision=HIGHEST,
         preferred_element_type=jnp.float32,
     )
-    full_s = lax.all_gather(search_raw, "mode", axis=2, tiled=True)
+    full_s = jnp.concatenate(
+        lax.all_to_all(jnp.stack([search_raw] * lax.axis_size("mode")), "mode", 0, 0), axis=2
+    )
     low_s, high_s = halo(full_s, CELLS)
     image_s = apply_dense(dense, low_s, full_s, high_s)
     flat_s = full_s.reshape(row_count, mode_count)

time: 348 us -> 360 us (1.034)
  blocking collectives: 11.1 us -> 43.5 us
  waiting for transfers between devices: 165 us -> 134 us
  local copies, waits for them, and re-layouts: 68.5 us -> 77.6 us
  starting transfers between devices: 30.3 us -> 36.3 us
    all_to_all x0 -> x1, blocking collectives: none -> 32.5 us  [local(): lax.all_to_all(jnp.stack([search_raw] * lax.axis_size('mode')), 'mode', 0...]
    all_gather x1 -> x0, waiting for transfers between devices: 26.9 us -> none  [local(): full_s = lax.all_gather(search_raw, 'mode', axis=2, tiled=True)]
    reshape x0 -> x3, local copies, waits for them, and re-layouts: none -> 10.1 us  [local(): jnp.concatenate(lax.all_to_all(jnp.stack([search_raw] * lax.axis_size('mo...]
    another operation x1 -> x4, local copies, waits for them, and re-layouts: 0.01 us -> 7.58 us  [the longest x2 7.3 us: local(): flat_s = full_s.reshape(row_count, mode_count)]
    ppermute x10, starting transfers between devices: 22.1 us -> 28.2 us  [space_sum(): value = value + lax.ppermute(value, 'space', pairs)]
    all_to_all x1, waiting for transfers between devices: 5.08 us -> 0.01 us  [apply_dense(): lax.all_to_all(total, 'mode', split_axis=2, concat_axis=1, tiled=True)]
    ppermute x2, waiting for transfers between devices: 0.01 us -> 4.47 us  [halo(): high = lax.ppermute(block[:width], 'space', backward)]
    ppermute x2, waiting for transfers between devices: 40.6 us -> 36.7 us  [halo(): low = lax.ppermute(block[block.shape[0] - width:], 'space', forward)]
  transfers between devices with their start and end apart: 17 -> 16, of which waited for: 15 -> 14; matrix products, arithmetic and copies ran while one was open for 14% -> 16% of each run, Pallas kernels for 0% -> 0%
where the time goes in v1:
time: 360 us; the launch traced here: 353 us
  waiting for transfers between devices  134 us (37%)
  local copies, waits for them, and re-layouts  77.6 us (22%)
  blocking collectives  43.5 us (12%)
  matrix products  36.9 us (10%)
  starting transfers between devices  36.3 us (10%)
  between operations  14.6 us (4%)
  other arithmetic  10.6 us (3%)
    ppermute x10, waiting for transfers between devices, space_sum(): value = value + lax.ppermute(value, 'space', pairs)  61 us
    ppermute x2, waiting for transfers between devices, halo(): low = lax.ppermute(block[block.shape[0] - width:], 'space', forward)  36.7 us
    all_to_all x1, blocking collectives, local(): lax.all_to_all(jnp.stack([search_raw] * lax.axis_size('mode')), 'mode', 0...  32.5 us
    all_gather x1, waiting for transfers between devices, local(): full_x = lax.all_gather(stacked_x, 'mode', axis=2, tiled=True)  31.6 us
    ppermute x10, starting transfers between devices, space_sum(): value = value + lax.ppermute(value, 'space', pairs)  28.2 us
    dot_general x6, matrix products, apply_dense(): jnp.einsum('ijrc,jcm->irm', coeffs, field, precision=HIGHEST, preferred_e...  23.6 us
    gather x2, local copies, waits for them, and re-layouts, dense_rows(): jnp.take(table, flat, axis=0).reshape(block_rows, ext_blocks, rows, cols)  14.9 us
    unnamed x36, local copies, waits for them, and re-layouts  13.2 us
  transfers between devices with their start and end apart: 16, of which 14 were waited for; matrix products, arithmetic and copies ran while one was open for 16% of the time, Pallas kernels for 0%

profile of v1, /device:TPU:2, one launch (start us, length us, event | category | flops | bytes accessed | tf_op | source)
XLA Modules:
  0.0 353.4 jit_solution(12955382183626039952)
XLA Ops:
  9.3 31.6 %all-gather.2.cloned.1.call-done = f32[9,192,256]{1,2,0:T(8,128)} async-done(((f32[9,192,32]{1,2,0:T(8,128)}), f32[9,192,256]{1,2,0:T(8,128)}) %all-gather.2.cloned.1.call-update) | async-done | bytes 1769488 | tf_op jit(solution)/shard_map/all_gather | solution.py:77
  44.6 6.7 %reshape.108 = f32[243,4608]{1,0:T(8,128)} reshape(f32[9,27,24,192]{3,2,1,0:T(8,128)} %param.5) | data formatting | bytes 8957952 | tf_op jit(solution)/shard_map/reshape | solution.py:38
  53.5 8.4 %gather_fusion = f32[243,4608]{1,0:T(8,128)} fusion(f32[243,4608]{1,0:T(8,128)} %reshape.108, s32[1024]{0:T(1024)S(1)} %pad_clamp_fusion), kind=kCustom, calls=%fused_computation | custom fusion | bytes 8958924 | tf_op jit(solution)/shard_map/jit(_take)/gather | solution.py:39
  61.9 6.5 %gather.7 = f32[9,27,24,192]{3,2,1,0:T(8,128)} reshape(f32[243,4608]{1,0:T(8,128)} %gather_fusion) | data formatting | bytes 8957952 | tf_op jit(solution)/shard_map/jit(_take)/gather | solution.py:39
  68.5 4.6 %fusion.16 = f32[9,24,256]{2,1,0:T(8,128)S(1)} fusion(f32[9,192,256]{1,2,0:T(8,128)} %all-gather.2.cloned.1.call-done, f32[9,27,24,192]{3,2,1,0:T(8,128)} %gather.7, pred[9,27]{1,0:T(8,128)(4,1)S(1)} %get-tuple-element.16, pred[9,27]{1,0:T(8,128)(4,1)S(1)} %fusion.44), kind=kOutput, calls=%fused_computation.24 | convolution fusion | flops 1148857344 | bytes 6470118 | tf_op jit(solution)/shard_map/ijrc,jcm->irm/dot_general | solution.py:53
  73.2 10.8 %collective-permute-done = f32[9,192,256]{2,1,0:T(8,128)} collective-permute-done((f32[9,192,256]{2,1,0:T(8,128)S(1)}, f32[9,192,256]{2,1,0:T(8,128)}, u32[]{:S(2)}, u32[]{:S(2)}) %collective-permute-start) | collective-permute-done | bytes 1769504 | tf_op jit(solution)/shard_map/ppermute | solution.py:24
  87.4 4.5 %collective-permute-done.1 = f32[9,192,256]{2,1,0:T(8,128)} collective-permute-done((f32[9,192,256]{2,1,0:T(8,128)S(1)}, f32[9,192,256]{2,1,0:T(8,128)}, u32[]{:S(2)}, u32[]{:S(2)}) %collective-permute-start.1) | collective-permute-done | bytes 1769504 | tf_op jit(solution)/shard_map/ppermute | solution.py:25
  91.9 4.2 %fusion.31 = f32[9,24,256]{2,1,0:T(8,128)} fusion(f32[9,24,256]{2,1,0:T(8,128)S(1)} %fusion.34, f32[9,192,256]{2,1,0:T(8,128)} %collective-permute-done.1, f32[9,27,24,192]{3,2,1,0:T(8,128)S(1)} %copy-done.2, pred[9,27]{1,0:T(8,128)(4,1)S(1)} %get-tuple-element.16, pred[9,27]{1,0:T(8,128)(4,1)S(1)} %fusion.44), kind=kOutput, calls=%fused_computation.29 | convolution fusion | flops 1148912640 | bytes 6691302 | tf_op jit(solution)/shard_map/ijrc,jcm->irm/dot_general | solution.py:53
  102.5 11.1 %all_to_all.35 = f32[8,1,6912]{2,1,0:T(1,128)} all-to-all(f32[8,1,6912]{2,1,0:T(1,128)} %reshape.140), channel_id=1, replica_groups=mesh['space'=32,'mode'=8] {'mode'}, dimensions={0} | all-to-all | bytes 442368 | tf_op jit(solution)/shard_map/all_to_all | solution.py:57
  141.7 4.7 %collective-permute-start.5 = (f32[256,32]{0,1:T(8,128)S(1)}, f32[256,32]{0,1:T(8,128)S(1)}, u32[]{:S(2)}, u32[]{:S(2)}) collective-permute-start(f32[256,32]{0,1:T(8,128)S(1)} %add.130), channel_id=1, source_target_pairs={{0,64},{8,72},{16,80},{24,88},{32,96},{40,104},{48,112},{56,120},{... | collective-permute-start | bytes 98312 | tf_op jit(solution)/shard_map/ppermute | solution.py:15
  152.1 4.0 %collective-permute-done.6 = f32[256,32]{0,1:T(8,128)S(1)} collective-permute-done((f32[256,32]{0,1:T(8,128)S(1)}, f32[256,32]{0,1:T(8,128)S(1)}, u32[]{:S(2)}, u32[]{:S(2)}) %collective-permute-start.6) | collective-permute-done | bytes 32800 | tf_op jit(solution)/shard_map/ppermute | solution.py:15
  161.5 32.5 %all_to_all.36 = f32[8,9,192,32]{2,3,1,0:T(8,128)S(1)} all-to-all(f32[8,9,192,32]{2,3,1,0:T(8,128)S(1)} %stack.8), channel_id=1, replica_groups=mesh['space'=32,'mode'=8] {'mode'}, dimensions={0} | all-to-all | bytes 3538944 | tf_op jit(solution)/shard_map/all_to_all | solution.py:101
  203.8 5.4 %copy.61 = f32[9,192,8,32]{1,0,3,2:T(8,128)} copy(f32[9,192,8,32]{1,3,0,2:T(8,128)} %bitcast.130) | data formatting | bytes 3538944 | tf_op jit(solution)/shard_map/reshape | solution.py:100
  209.2 4.5 %fusion.15 = f32[9,24,256]{2,1,0:T(8,128)S(1)} fusion(f32[9,192,256,1]{1,2,0,3:T(8,128)} %bitcast.135, f32[9,27,24,192]{3,2,1,0:T(8,128)} %gather.7, pred[9,27]{1,0:T(8,128)(4,1)S(1)} %get-tuple-element.16, pred[9,27]{1,0:T(8,128)(4,1)S(1)} %fusion.44), kind=kOutput, calls=%fused_computation.23 | convolution fusion | flops 1148857344 | bytes 6470118 | tf_op jit(solution)/shard_map/ijrc,jcm->irm/dot_general | solution.py:53
  213.6 25.9 %collective-permute-done.7 = f32[9,192,256]{2,1,0:T(8,128)} collective-permute-done((f32[9,192,256]{2,1,0:T(8,128)}, f32[9,192,256]{2,1,0:T(8,128)}, u32[]{:S(2)}, u32[]{:S(2)}) %collective-permute-start.7) | collective-permute-done | bytes 1769504 | tf_op jit(solution)/shard_map/ppermute | solution.py:24
  257.6 4.6 %reshape_reshape.3 = f32[1728,256]{0,1:T(8,128)} reshape(f32[9,192,8,32]{1,0,3,2:T(8,128)} %copy.61) | data formatting | bytes 3538944 | tf_op jit(solution)/shard_map/reshape;reshape | solution.py:105
  272.5 7.3 %convolution_bitcast_fusion = f32[65536]{0:T(1024)S(1)} fusion(f32[1728,128]{0,1:T(8,128)S(1)} %bitcast.144, f32[1728,256]{1,0:T(8,128)} %copy.62, f32[1728,256]{1,0:T(8,128)S(1)} %bitcast.133), kind=kOutput, calls=%fused_computation.1 | convolution fusion | flops 1359839232 | bytes 4685824
  279.9 5.5 %collective-permute-start.9 = (f32[65792]{0:T(1024)S(1)}, f32[65792]{0:T(1024)S(1)}, u32[]{:S(2)}, u32[]{:S(2)}) collective-permute-start(f32[65792]{0:T(1024)S(1)} %pad_maximum_fusion.1), channel_id=1, source_target_pairs={{0,8},{8,0},{16,24},{24,16},{32,40},{40,32},{48,56},{56,48},{64,72... | collective-permute-start | bytes 789512 | tf_op jit(solution)/shard_map/ppermute | solution.py:15
  285.4 7.0 %collective-permute-done.9 = f32[65792]{0:T(1024)S(1)} collective-permute-done((f32[65792]{0:T(1024)S(1)}, f32[65792]{0:T(1024)S(1)}, u32[]{:S(2)}, u32[]{:S(2)}) %collective-permute-start.9) | collective-permute-done | bytes 263200 | tf_op jit(solution)/shard_map/ppermute | solution.py:15
  292.5 9.7 %collective-permute-done.10 = f32[65792]{0:T(1024)S(1)} collective-permute-done((f32[65792]{0:T(1024)S(1)}, f32[65792]{0:T(1024)S(1)}, u32[]{:S(2)}, u32[]{:S(2)}) %collective-permute-start.10) | collective-permute-done | bytes 263200 | tf_op jit(solution)/shard_map/ppermute | solution.py:15
  302.3 7.3 %collective-permute-done.11 = f32[65792]{0:T(1024)S(1)} collective-permute-done((f32[65792]{0:T(1024)S(1)}, f32[65792]{0:T(1024)S(1)}, u32[]{:S(2)}, u32[]{:S(2)}) %collective-permute-start.11) | collective-permute-done | bytes 263200 | tf_op jit(solution)/shard_map/ppermute | solution.py:15
  310.7 12.1 %collective-permute-done.12 = f32[65792]{0:T(1024)S(1)} collective-permute-done((f32[65792]{0:T(1024)S(1)}, f32[65792]{0:T(1024)S(1)}, u32[]{:S(2)}, u32[]{:S(2)}) %collective-permute-start.12) | collective-permute-done | bytes 263200 | tf_op jit(solution)/shard_map/ppermute | solution.py:15
  322.8 4.7 %collective-permute-start.13 = (f32[65792]{0:T(1024)S(1)}, f32[65792]{0:T(1024)S(1)}, u32[]{:S(2)}, u32[]{:S(2)}) collective-permute-start(f32[65792]{0:T(1024)S(1)} %add.138), channel_id=1, source_target_pairs={{0,128},{8,136},{16,144},{24,152},{32,160},{40,168},{48,176},{56,1... | collective-permute-start | bytes 789512 | tf_op jit(solution)/shard_map/ppermute | solution.py:15
  328.0 13.1 %collective-permute-done.13 = f32[65792]{0:T(1024)S(1)} collective-permute-done((f32[65792]{0:T(1024)S(1)}, f32[65792]{0:T(1024)S(1)}, u32[]{:S(2)}, u32[]{:S(2)}) %collective-permute-start.13) | collective-permute-done | bytes 263200 | tf_op jit(solution)/shard_map/ppermute | solution.py:15
  (117 shorter events, 102.2 us)
Async XLA Ops:
  7.2 152.3 %copy-start = (f32[9,192,192]{2,1,0:T(8,128)S(1)}, f32[9,192,192]{2,1,0:T(8,128)}, u32[]{:S(2)}) copy-start(f32[9,192,192]{2,1,0:T(8,128)} %param.6) | copy-start | bytes 3981316
  7.2 33.8 %all-gather.2.cloned.1.call-start = ((), (), s32[]{:S(2)}) async-start(), calls=%async_computation.3 | async-start | bytes 2654208 | tf_op jit(solution)/shard_map/all_gather | solution.py:77
  43.0 113.1 %copy-start.4 = (f32[9,192,256]{2,1,0:T(8,128)}, f32[9,192,256]{2,1,0:T(8,128)S(1)}, u32[]{:S(2)}) copy-start(f32[9,192,256]{2,1,0:T(8,128)S(1)} %copy.54) | copy-start | bytes 5308420
  43.0 40.9 %collective-permute-start = (f32[9,192,256]{2,1,0:T(8,128)S(1)}, f32[9,192,256]{2,1,0:T(8,128)}, u32[]{:S(2)}, u32[]{:S(2)}) collective-permute-start(f32[9,192,256]{2,1,0:T(8,128)S(1)} %copy.54), channel_id=1, source_target_pairs={{0,8},{8,16},{16,24},{24,32},{32,40},{40,48},{48,56},{56,64},{64,7... | collective-permute-start | bytes 5308424 | tf_op jit(solution)/shard_map/ppermute | solution.py:24
  44.6 7.3 %copy-start.12 = (s32[9,27]{1,0:T(8,128)S(1)}, s32[9,27]{1,0:T(8,128)}, u32[]{:S(2)}) copy-start(s32[9,27]{1,0:T(8,128)} %param.7) | copy-start | bytes 2920
  51.3 40.6 %collective-permute-start.1 = (f32[9,192,256]{2,1,0:T(8,128)S(1)}, f32[9,192,256]{2,1,0:T(8,128)}, u32[]{:S(2)}, u32[]{:S(2)}) collective-permute-start(f32[9,192,256]{2,1,0:T(8,128)S(1)} %copy.54), channel_id=1, source_target_pairs={{8,0},{16,8},{24,16},{32,24},{40,32},{48,40},{56,48},{64,56},{72,6... | collective-permute-start | bytes 5308424 | tf_op jit(solution)/shard_map/ppermute | solution.py:25
  68.5 15.4 %copy-start.2 = (f32[9,27,24,192]{3,2,1,0:T(8,128)S(1)}, f32[9,27,24,192]{3,2,1,0:T(8,128)}, u32[]{:S(2)}) copy-start(f32[9,27,24,192]{3,2,1,0:T(8,128)} %gather.7) | copy-start | bytes 13436932
  125.4 30.7 %copy-start.9 = (f32[1728,32]{0,1:T(8,128)S(1)}, f32[1728,32]{0,1:T(8,128)}, u32[]{:S(2)}) copy-start(f32[1728,32]{0,1:T(8,128)} %reshape.110) | copy-start | bytes 663556
  127.4 5.0 %collective-permute-start.2 = (f32[256,32]{0,1:T(8,128)S(1)}, f32[256,32]{0,1:T(8,128)S(1)}, u32[]{:S(2)}, u32[]{:S(2)}) collective-permute-start(f32[256,32]{0,1:T(8,128)S(1)} %convolution_bitcast_fusion.3), channel_id=1, source_target_pairs={{0,8},{8,0},{16,24},{24,16},{32,40},{40,32},{48,56},{56,48},{64,72... | collective-permute-start | bytes 98312 | tf_op jit(solution)/shard_map/ppermute | solution.py:15
  132.4 5.4 %collective-permute-start.3 = (f32[256,32]{0,1:T(8,128)S(1)}, f32[256,32]{0,1:T(8,128)S(1)}, u32[]{:S(2)}, u32[]{:S(2)}) collective-permute-start(f32[256,32]{0,1:T(8,128)S(1)} %add.128), channel_id=1, source_target_pairs={{0,16},{8,24},{16,0},{24,8},{32,48},{40,56},{48,32},{56,40},{64,80... | collective-permute-start | bytes 98312 | tf_op jit(solution)/shard_map/ppermute | solution.py:15
  137.8 3.9 %collective-permute-start.4 = (f32[256,32]{0,1:T(8,128)S(1)}, f32[256,32]{0,1:T(8,128)S(1)}, u32[]{:S(2)}, u32[]{:S(2)}) collective-permute-start(f32[256,32]{0,1:T(8,128)S(1)} %add.129), channel_id=1, source_target_pairs={{0,32},{8,40},{16,48},{24,56},{32,0},{40,8},{48,16},{56,24},{64,96... | collective-permute-start | bytes 98312 | tf_op jit(solution)/shard_map/ppermute | solution.py:15
  141.7 6.6 %collective-permute-start.5 = (f32[256,32]{0,1:T(8,128)S(1)}, f32[256,32]{0,1:T(8,128)S(1)}, u32[]{:S(2)}, u32[]{:S(2)}) collective-permute-start(f32[256,32]{0,1:T(8,128)S(1)} %add.130), channel_id=1, source_target_pairs={{0,64},{8,72},{16,80},{24,88},{32,96},{40,104},{48,112},{56,120},{... | collective-permute-start | bytes 98312 | tf_op jit(solution)/shard_map/ppermute | solution.py:15
  148.3 7.8 %collective-permute-start.6 = (f32[256,32]{0,1:T(8,128)S(1)}, f32[256,32]{0,1:T(8,128)S(1)}, u32[]{:S(2)}, u32[]{:S(2)}) collective-permute-start(f32[256,32]{0,1:T(8,128)S(1)} %add.131), channel_id=1, source_target_pairs={{0,128},{8,136},{16,144},{24,152},{32,160},{40,168},{48,176},{56,1... | collective-permute-start | bytes 98312 | tf_op jit(solution)/shard_map/ppermute | solution.py:15
  199.3 40.3 %collective-permute-start.7 = (f32[9,192,256]{2,1,0:T(8,128)}, f32[9,192,256]{2,1,0:T(8,128)}, u32[]{:S(2)}, u32[]{:S(2)}) collective-permute-start(f32[9,192,256]{2,1,0:T(8,128)} %copy.66), channel_id=1, source_target_pairs={{0,8},{8,16},{16,24},{24,32},{32,40},{40,48},{48,56},{56,64},{64,7... | collective-permute-start | bytes 5308424 | tf_op jit(solution)/shard_map/ppermute | solution.py:24
  201.1 41.9 %collective-permute-start.8 = (f32[9,192,256]{2,1,0:T(8,128)}, f32[9,192,256]{2,1,0:T(8,128)}, u32[]{:S(2)}, u32[]{:S(2)}) collective-permute-start(f32[9,192,256]{2,1,0:T(8,128)} %copy.66), channel_id=1, source_target_pairs={{8,0},{16,8},{24,16},{32,24},{40,32},{48,40},{56,48},{64,56},{72,6... | collective-permute-start | bytes 5308424 | tf_op jit(solution)/shard_map/ppermute | solution.py:25
  203.0 36.6 %slice-start = ((s8[5971968]{0:T(1024)(128)(4,1)}), s8[1777664]{0:T(1024)(128)(4,1)S(1)}, s32[]{:S(2)}) async-start(s8[5971968]{0:T(1024)(128)(4,1)} %bitcast.127), calls=%async_computation.4 | async-start | bytes 3555328
  203.8 35.8 %slice-start.1 = ((s8[5971968]{0:T(1024)(128)(4,1)}), s8[4194304]{0:T(1024)(128)(4,1)S(1)}, s32[]{:S(2)}) async-start(s8[5971968]{0:T(1024)(128)(4,1)} %bitcast.127), calls=%async_computation.5 | async-start | bytes 8388608
  252.0 12.9 %all-to-all-start.2 = ((f32[8,1,6912]{2,1,0:T(1,128)}), f32[8,1,6912]{2,1,0:T(1,128)S(1)}, u32[]{:S(2)}, u32[]{:S(2)}) async-start(f32[8,1,6912]{2,1,0:T(1,128)} %reshape.142), calls=%async_computation.2 | async-start | bytes 442368 | tf_op jit(solution)/shard_map/all_to_all | solution.py:57
  279.9 47.6 %copy-start.8 = (f32[9,192,32]{1,0,2:T(8,128)S(1)}, f32[9,192,32]{1,0,2:T(8,128)}, u32[]{:S(2)}) copy-start(f32[9,192,32]{1,0,2:T(8,128)} %copy-done.7) | copy-start | bytes 663556
  279.9 12.5 %collective-permute-start.9 = (f32[65792]{0:T(1024)S(1)}, f32[65792]{0:T(1024)S(1)}, u32[]{:S(2)}, u32[]{:S(2)}) collective-permute-start(f32[65792]{0:T(1024)S(1)} %pad_maximum_fusion.1), channel_id=1, source_target_pairs={{0,8},{8,0},{16,24},{24,16},{32,40},{40,32},{48,56},{56,48},{64,72... | collective-permute-start | bytes 789512 | tf_op jit(solution)/shard_map/ppermute | solution.py:15
  292.4 9.8 %collective-permute-start.10 = (f32[65792]{0:T(1024)S(1)}, f32[65792]{0:T(1024)S(1)}, u32[]{:S(2)}, u32[]{:S(2)}) collective-permute-start(f32[65792]{0:T(1024)S(1)} %fusion.70), channel_id=1, source_target_pairs={{0,16},{8,24},{16,0},{24,8},{32,48},{40,56},{48,32},{56,40},{64,80... | collective-permute-start | bytes 789512 | tf_op jit(solution)/shard_map/ppermute | solution.py:15
  302.2 7.4 %collective-permute-start.11 = (f32[65792]{0:T(1024)S(1)}, f32[65792]{0:T(1024)S(1)}, u32[]{:S(2)}, u32[]{:S(2)}) collective-permute-start(f32[65792]{0:T(1024)S(1)} %add.136), channel_id=1, source_target_pairs={{0,32},{8,40},{16,48},{24,56},{32,0},{40,8},{48,16},{56,24},{64,96... | collective-permute-start | bytes 789512 | tf_op jit(solution)/shard_map/ppermute | solution.py:15
  309.6 13.1 %collective-permute-start.12 = (f32[65792]{0:T(1024)S(1)}, f32[65792]{0:T(1024)S(1)}, u32[]{:S(2)}, u32[]{:S(2)}) collective-permute-start(f32[65792]{0:T(1024)S(1)} %add.137), channel_id=1, source_target_pairs={{0,64},{8,72},{16,80},{24,88},{32,96},{40,104},{48,112},{56,120},{... | collective-permute-start | bytes 789512 | tf_op jit(solution)/shard_map/ppermute | solution.py:15
  322.8 18.3 %collective-permute-start.13 = (f32[65792]{0:T(1024)S(1)}, f32[65792]{0:T(1024)S(1)}, u32[]{:S(2)}, u32[]{:S(2)}) collective-permute-start(f32[65792]{0:T(1024)S(1)} %add.138), channel_id=1, source_target_pairs={{0,128},{8,136},{16,144},{24,152},{32,160},{40,168},{48,176},{56,1... | collective-permute-start | bytes 789512 | tf_op jit(solution)/shard_map/ppermute | solution.py:15
  (7 other events, 27.4 us)
Sparse Core Ops, SparseCore 0:
  9.8 31.0 all-gather.1
